TPU v7x, 32 devices: a whole 2x2x4 slice. The times are simulated.
32 devices in a mesh: rep: 2 (over x), tm: 8 (over z, y), mp: 2 (over core).
Axes of the slice: x: 2, y: 2, z: 4, core: 2. Of those that a mesh axis runs over, the one named last changes fastest.
Arguments:
- inputs: bfloat16 [8, 1024, 1024], P('rep', 'tm'), parts along dimension 0, may hold values from -6 to 6
- resets: int32 [8, 1024], P('rep', 'tm'), parts along dimension 0, may hold values 0 or 1
- actions: int32 [8, 8, 128, 4], P('rep', None, 'tm'), parts along dimension 0, may hold values from 0 to 17
- in_proj: bfloat16 [1024, 1024], P(None, 'mp'), may hold values from -0.1875 to 0.1875
- decay_rates: float32 [1024], replicated, may hold values from 0.00024414062 to 0.03
- readout_w: bfloat16 [1024, 1024], P('mp'), may hold values from -0.1875 to 0.1875
- norm_gain: float32 [1024], replicated, may hold values from 0.1 to 1.9
- w_hidden: bfloat16 [1024, 1024], P(None, 'mp'), may hold values from -0.1875 to 0.1875
- action_embed: bfloat16 [18, 1024], P(None, 'mp'), may hold values from -6 to 6
- w_out: bfloat16 [1024, 1024], P('mp'), may hold values from -0.1875 to 0.1875
Outputs:
- predicted: bfloat16 [8, 8, 128, 4, 1024], P('rep', None, 'tm', None, 'mp'), parts along dimension 0
There are 2 independent parts, one for each index of `rep`. A program takes and returns all parts, laid end to end along the dimension named above; an argument that names none is the same for every part. Nothing has to cross between parts.
All inputs are finite; a program needn't handle non-finite values. No bound on the sum of `resets` on one device may be relied on, other than what follows from the above.
Results may differ from a plain program's by a relative error of at most 0.015.
Values may be sent and summed in bfloat16 or wider, within the bound.
No kernel may reach another device: no remote copies, remote signals or barrier semaphores. Data moves between devices by JAX's collectives and lax.ppermute only.
A program may use at most 64 MiB of HBM per device.

v0:
```python
import jax
import jax.numpy as jnp
from jax import lax
from jax.sharding import PartitionSpec as P


def carried_in(value, axis, join, neutral):
    count, mine = (lax.axis_size(axis), lax.axis_index(axis))
    pieces = jax.tree.map(lambda part: lax.all_gather(part, axis), value)
    total = jax.tree.map(
        lambda part, zero: jnp.full_like(part, 0) + jnp.asarray(zero, part.dtype), value, neutral
    )

    def hop(position, total):
        longer = join(total, jax.tree.map(lambda part: part[position], pieces))
        return jax.tree.map(lambda new, old: jnp.where(position < mine, new, old), longer, total)

    return lax.fori_loop(0, count - 1, hop, total)


def shortened(value):

    def short(part):
        return part.astype(jnp.bfloat16) if part.dtype == jnp.float32 else part

    return jax.tree.map(short, value)


def combine(earlier, later):
    return (earlier[0] * later[0], later[0] * earlier[1] + later[1])


def hidden_units(features, norm_gain, w_hidden, action_embed, picked):
    mean_sq = jnp.mean(features * features, axis=-1, keepdims=True)
    normed = (features * lax.rsqrt(mean_sq + 1e-06) * norm_gain).astype(jnp.bfloat16)
    table_ids = jnp.arange(action_embed.shape[0], dtype=jnp.int32)
    one_hot = (picked[:, None] == table_ids[None, :]).astype(jnp.bfloat16)
    pre_act = jnp.dot(normed, w_hidden, preferred_element_type=jnp.float32) + jnp.dot(
        one_hot, action_embed, preferred_element_type=jnp.float32
    )
    return jax.nn.silu(pre_act).astype(jnp.bfloat16)


def per_device(
    inputs,
    resets,
    actions,
    in_proj,
    decay_rates,
    readout_w,
    norm_gain,
    w_hidden,
    action_embed,
    w_out,
):
    mp_index = lax.axis_index("mp")
    width_part = in_proj.shape[1]
    local_rates = lax.dynamic_slice_in_dim(decay_rates, mp_index * width_part, width_part)
    decays = jnp.exp(-local_rates)
    scaling = jnp.sqrt(1.0 - decays * decays)
    batch, steps, width = inputs.shape
    driven = (
        jnp.dot(
            inputs.reshape(batch * steps, width), in_proj, preferred_element_type=jnp.float32
        ).reshape(batch, steps, width_part)
        * scaling
    )
    keep_mask = (1 - resets).astype(jnp.float32)
    gates = keep_mask[:, :, None] * decays
    cumulative, local_states = lax.associative_scan(combine, (gates, driven), axis=1)
    identity = (
        jnp.ones((batch, width_part), jnp.float32),
        jnp.zeros((batch, width_part), jnp.float32),
    )
    entering = carried_in((cumulative[:, -1], local_states[:, -1]), "tm", combine, identity)
    carry_state = entering[1]
    corrected = local_states + cumulative * carry_state[:, None, :]
    posterior = lax.all_to_all(
        shortened(corrected.reshape(batch, 1, steps, width_part)),
        "tm",
        split_axis=2,
        concat_axis=1,
        tiled=True,
    )
    seqs, blocks, sub_steps, horizon = actions.shape
    rows = seqs * blocks * sub_steps
    current = posterior.reshape(rows, width_part)
    action_rows = actions.reshape(rows, horizon)
    outputs = []
    for step in range(horizon):
        features = lax.psum(
            jnp.dot(
                current.astype(jnp.bfloat16), readout_w, preferred_element_type=jnp.float32
            ).astype(jnp.bfloat16),
            "mp",
        ).astype(jnp.float32)
        hidden = hidden_units(features, norm_gain, w_hidden, action_embed, action_rows[:, step])
        guessed = lax.psum_scatter(
            jnp.dot(hidden, w_out, preferred_element_type=jnp.float32).astype(jnp.bfloat16),
            "mp",
            scatter_dimension=1,
            tiled=True,
        )
        outputs.append(guessed)
        if step < horizon - 1:
            full_guess = lax.all_gather(guessed, "mp", axis=1, tiled=True)
            current = decays * current + scaling * jnp.dot(
                full_guess, in_proj, preferred_element_type=jnp.float32
            )
    result = jnp.stack(outputs, axis=1)
    return result.reshape(seqs, blocks, sub_steps, horizon, result.shape[2])


def solution(mesh):
    in_specs = (
        P("rep", "tm", None),
        P("rep", "tm"),
        P("rep", None, "tm", None),
        P(None, "mp"),
        P(),
        P("mp", None),
        P(),
        P(None, "mp"),
        P(None, "mp"),
        P("mp", None),
    )
    out_specs = P("rep", None, "tm", None, "mp")
    return jax.shard_map(
        per_device, mesh=mesh, in_specs=in_specs, out_specs=out_specs, check_vma=False
    )
```

profile of v0, /device:TPU:0, one launch (start us, length us, event | category | flops | bytes accessed | tf_op | source)
XLA Modules:
  0.0 339.0 jit_solution(1014321069220786846)
XLA Ops:
  6.5 0.8 subtract_convert_fusion
  7.3 0.8 subtract_sqrt_fusion
  8.2 0.3 slice.224
  8.5 0.3 slice.220
  8.8 1.5 slice.219
  10.3 2.2 convolution_multiply_fusion.3
  12.6 1.5 slice.268
  14.1 1.5 slice.222
  15.6 1.5 slice.221
  17.1 1.4 multiply_add_fusion
  19.3 0.8 slice.225
  22.9 0.5 copy-done.9
  24.2 0.9 add.280
  25.0 0.9 add.272
  25.9 1.2 fusion.36
  27.1 0.2 pad.112
  27.4 0.7 copy-done.6
  28.1 0.9 pad_maximum_fusion.1
  29.0 2.0 pad.98
  31.0 4.3 %pad.99 = f32[4,128,512]{2,1,0:T(8,128)} pad(f32[4,64,512]{2,1,0:T(8,128)} %add.272, f32[]{:T(128)} %constant.52.clone.1), padding=0_0_0x1_0_1x0_0_0 | pad | bytes 1572868 | tf_op jit(solution)/shard_map/pad | solution.py:70
  35.3 0.9 slice_add_fusion
  36.2 32.4 %all-gather.1 = f32[32,1,512]{2,1,0:T(1,128)S(1)} all-gather(f32[4,1,512]{2,1,0:T(1,128)S(1)} %slice_add_fusion), channel_id=3, replica_groups=mesh['rep'=2,'tm'=8,'mp'=2] {'tm'}, dimensions={0}, use_global_device_ids=true | all-gather | bytes 73728 | tf_op jit(solution)/shard_map/all_gather | solution.py:9
  68.7 4.3 %pad.113 = f32[4,128,512]{2,1,0:T(8,128)} pad(f32[4,64,512]{2,1,0:T(8,128)} %add.280, f32[]{:T(128)} %constant.52.clone.1), padding=0_0_0x1_0_1x0_0_0 | pad | bytes 1572868 | tf_op jit(solution)/shard_map/pad | solution.py:70
  73.0 0.9 slice_add_fusion.1
  73.8 30.7 %all-gather = f32[32,1,512]{2,1,0:T(1,128)S(1)} all-gather(f32[4,1,512]{2,1,0:T(1,128)S(1)} %slice_add_fusion.1), channel_id=2, replica_groups=mesh['rep'=2,'tm'=8,'mp'=2] {'tm'}, dimensions={0}, use_global_device_ids=true | all-gather | bytes 73728 | tf_op jit(solution)/shard_map/all_gather | solution.py:9
  104.7 0.3 while.14
  105.0 2.0 fusion.35
  107.1 0.4 copy.20
  107.5 15.5 %all_to_all.4 = bf16[4,1,128,512]{3,0,1,2:T(4,128)(2,1)S(1)} all-to-all(bf16[4,1,128,512]{3,0,1,2:T(4,128)(2,1)S(1)} %copy.20), channel_id=1, replica_groups=mesh['rep'=2,'tm'=8,'mp'=2] {'tm'}, dimensions={2} | all-to-all | bytes 1048576 | tf_op jit(solution)/shard_map/all_to_all | solution.py:78
  123.1 0.8 copy-done.10
  123.9 1.7 convolution_convert_fusion.7
  125.7 18.4 %all-reduce.33.cloned.1.call-done = bf16[512,1024]{1,0:T(8,128)(2,1)} async-done(((bf16[512,1024]{1,0:T(8,128)(2,1)}), bf16[512,1024]{1,0:T(8,128)(2,1)}) %all-reduce.33.cloned.1.call-update) | async-done | bytes 1048592 | tf_op jit(solution)/shard_map/psum | solution.py:91
  144.1 1.5 fusion.1
  145.7 3.0 fusion.23
  148.6 3.7 %convolution_convert_fusion.6 = bf16[512,1024]{1,0:T(8,128)(2,1)} fusion(bf16[512,1024]{1,0:T(8,128)(2,1)} %param.21, f32[512,512]{1,0:T(8,128)} %fusion.23, bf16[18,512]{1,0:T(8,128)(2,1)S(1)} %copy-done.16, s32[512]{0:T(512)S(1)} %bitcast.91), kind=kOutput, calls=%fused_computation.30 | convolution fusion | flops 548414464 | bytes 3166208 | tf_op jit(solution)/shard_map/dot_general | solution.py:99
  152.4 9.7 %reduce-scatter.5.cloned.1.call-done = bf16[512,512]{1,0:T(8,128)(2,1)} async-done(((bf16[512,1024]{1,0:T(8,128)(2,1)}), bf16[512,512]{1,0:T(8,128)(2,1)}) %reduce-scatter.5.cloned.1.call-update) | async-done | bytes 524304 | tf_op jit(solution)/shard_map/reduce_scatter | solution.py:98
  162.1 11.7 %all-gather.6.cloned.1.call-done = bf16[512,1024]{1,0:T(8,128)(2,1)} async-done(((bf16[512,512]{1,0:T(8,128)(2,1)}), bf16[512,1024]{1,0:T(8,128)(2,1)}) %all-gather.6.cloned.1.call-update) | async-done | bytes 1048592 | tf_op jit(solution)/shard_map/all_gather | solution.py:106
  173.9 2.1 fusion.15
  175.9 1.7 convolution_convert_fusion.5
  177.9 20.5 %all-reduce.35.cloned.1.call-done = bf16[512,1024]{1,0:T(8,128)(2,1)} async-done(((bf16[512,1024]{1,0:T(8,128)(2,1)}), bf16[512,1024]{1,0:T(8,128)(2,1)}) %all-reduce.35.cloned.1.call-update) | async-done | bytes 1048592 | tf_op jit(solution)/shard_map/psum | solution.py:91
  198.4 1.5 fusion.4
  199.9 3.0 fusion.21
  202.9 3.6 %convolution_convert_fusion.4 = bf16[512,1024]{1,0:T(8,128)(2,1)} fusion(bf16[512,1024]{1,0:T(8,128)(2,1)} %param.21, f32[512,512]{1,0:T(8,128)} %fusion.21, bf16[18,512]{1,0:T(8,128)(2,1)S(1)} %copy-done.16, s32[512]{0:T(512)S(1)} %bitcast.90), kind=kOutput, calls=%fused_computation.28 | convolution fusion | flops 548414464 | bytes 3166208 | tf_op jit(solution)/shard_map/dot_general | solution.py:99
  206.5 9.7 %reduce-scatter.7.cloned.1.call-done = bf16[512,512]{1,0:T(8,128)(2,1)} async-done(((bf16[512,1024]{1,0:T(8,128)(2,1)}), bf16[512,512]{1,0:T(8,128)(2,1)}) %reduce-scatter.7.cloned.1.call-update) | async-done | bytes 524304 | tf_op jit(solution)/shard_map/reduce_scatter | solution.py:98
  216.3 11.6 %all-gather.8.cloned.1.call-done = bf16[512,1024]{1,0:T(8,128)(2,1)} async-done(((bf16[512,512]{1,0:T(8,128)(2,1)}), bf16[512,1024]{1,0:T(8,128)(2,1)}) %all-gather.8.cloned.1.call-update) | async-done | bytes 1048592 | tf_op jit(solution)/shard_map/all_gather | solution.py:106
  227.9 2.2 fusion.14
  230.1 1.7 convolution_convert_fusion.3
  231.9 20.7 %all-reduce.37.cloned.1.call-done = bf16[512,1024]{1,0:T(8,128)(2,1)} async-done(((bf16[512,1024]{1,0:T(8,128)(2,1)}), bf16[512,1024]{1,0:T(8,128)(2,1)}) %all-reduce.37.cloned.1.call-update) | async-done | bytes 1048592 | tf_op jit(solution)/shard_map/psum | solution.py:91
  252.6 1.5 fusion.7
  254.1 3.0 fusion.19
  257.1 3.7 %convolution_convert_fusion.2 = bf16[512,1024]{1,0:T(8,128)(2,1)} fusion(bf16[512,1024]{1,0:T(8,128)(2,1)} %param.21, f32[512,512]{1,0:T(8,128)} %fusion.19, bf16[18,512]{1,0:T(8,128)(2,1)S(1)} %copy-done.16, s32[512]{0:T(512)S(1)} %bitcast.89), kind=kOutput, calls=%fused_computation.26 | convolution fusion | flops 548414464 | bytes 3166208 | tf_op jit(solution)/shard_map/dot_general | solution.py:99
  260.8 9.7 %reduce-scatter.9.cloned.1.call-done = bf16[512,512]{1,0:T(8,128)(2,1)} async-done(((bf16[512,1024]{1,0:T(8,128)(2,1)}), bf16[512,512]{1,0:T(8,128)(2,1)}) %reduce-scatter.9.cloned.1.call-update) | async-done | bytes 524304 | tf_op jit(solution)/shard_map/reduce_scatter | solution.py:98
  270.6 11.7 %all-gather.10.cloned.1.call-done = bf16[512,1024]{1,0:T(8,128)(2,1)} async-done(((bf16[512,512]{1,0:T(8,128)(2,1)}), bf16[512,1024]{1,0:T(8,128)(2,1)}) %all-gather.10.cloned.1.call-update) | async-done | bytes 1048592 | tf_op jit(solution)/shard_map/all_gather | solution.py:106
  282.3 3.5 %convolution_convert_fusion.1 = bf16[512,1024]{1,0:T(8,128)(2,1)} fusion(bf16[512,1024]{1,0:T(8,128)(2,1)S(1)} %copy-done, bf16[512,1024]{1,0:T(8,128)(2,1)} %all-gather.10.cloned.1.call-done, bf16[1024,512]{1,0:T(8,128)(2,1)S(1)} %copy-done.8, f32[512,512]{1,0:T(8,128)S(1)} %fusion.14, f32[512]{0:T(512)S(1)} %get-tuple-element.128, ...), kind=kOutput, calls=%fused_computation.25 | convolution fusion | flops 1075314688 | bytes 5246976 | tf_op jit(solution)/shard_map/dot_general | solution.py:92
  285.8 20.7 %all-reduce.39.cloned.1.call-done = bf16[512,1024]{1,0:T(8,128)(2,1)} async-done(((bf16[512,1024]{1,0:T(8,128)(2,1)}), bf16[512,1024]{1,0:T(8,128)(2,1)}) %all-reduce.39.cloned.1.call-update) | async-done | bytes 1048592 | tf_op jit(solution)/shard_map/psum | solution.py:91
  306.5 1.5 fusion.10
  308.0 3.0 fusion.17
  311.0 3.7 %convolution_convert_fusion = bf16[512,1024]{1,0:T(8,128)(2,1)} fusion(bf16[512,1024]{1,0:T(8,128)(2,1)} %param.21, f32[512,512]{1,0:T(8,128)} %fusion.17, bf16[18,512]{1,0:T(8,128)(2,1)S(1)} %copy-done.16, s32[512]{0:T(512)S(1)} %bitcast.88), kind=kOutput, calls=%fused_computation.24 | convolution fusion | flops 548414464 | bytes 3166208 | tf_op jit(solution)/shard_map/dot_general | solution.py:99
  314.7 1.0 copy.23
  315.7 2.1 copy.24
  317.8 2.0 copy.25
  319.9 4.5 %reduce-scatter.11.cloned.1.call-done = bf16[512,512]{1,0:T(8,128)(2,1)} async-done(((bf16[512,1024]{1,0:T(8,128)(2,1)}), bf16[512,512]{1,0:T(8,128)(2,1)}) %reduce-scatter.11.cloned.1.call-update) | async-done | bytes 524304 | tf_op jit(solution)/shard_map/reduce_scatter | solution.py:98
  324.4 2.2 copy.26
  326.6 5.9 %pad_maximum_fusion = bf16[4,8,16,4,512]{4,3,2,1,0:T(4,128)(2,1)} fusion(bf16[4,8,16,1,512]{4,3,2,1,0:T(2,128)(2,1)S(1)} %copy.26, bf16[4,8,16,1,512]{4,3,2,1,0:T(2,128)(2,1)S(1)} %copy-done.1, bf16[4,8,16,1,512]{4,3,2,1,0:T(2,128)(2,1)S(1)} %copy.24, bf16[4,8,16,1,512]{4,3,2,1,0:T(2,128)(2,1)S(1)} %copy.23), kind=kLoop, calls=%fused_computation.23 | loop fusion | flops 8388608 | bytes 4194304 | tf_op jit(solution)/shard_map/stack | solution.py:110
  (163 shorter events, 5.7 us)
Async XLA Ops:
  6.5 117.3 %copy-start = (bf16[512,1024]{1,0:T(8,128)(2,1)S(1)}, bf16[512,1024]{1,0:T(8,128)(2,1)}, u32[]{:S(2)}) copy-start(bf16[512,1024]{1,0:T(8,128)(2,1)} %param.17) | copy-start | bytes 3145732
  6.5 137.6 %all-reduce.33.cloned.1.call-start = ((), (), s32[]{:S(2)}) async-start(), calls=%async_computation.5 | async-start | bytes 2097152 | tf_op jit(solution)/shard_map/psum | solution.py:91
  22.4 1.0 copy-start.9
  24.1 1.8 copy-start.4
  24.1 1.8 copy-start.5
  27.1 1.0 copy-start.6
  123.1 0.8 copy-start.10
  123.1 2.5 copy-start.11
  123.8 21.8 %copy-start.12 = (bf16[1024,512]{1,0:T(8,128)(2,1)S(1)}, bf16[1024,512]{1,0:T(8,128)(2,1)}, u32[]{:S(2)}) copy-start(bf16[1024,512]{1,0:T(8,128)(2,1)} %param.19) | copy-start | bytes 3145732
  123.9 21.8 %copy-start.17 = (f32[1024]{0:T(1024)S(1)}, f32[1024]{0:T(1024)}, u32[]{:S(2)}) copy-start(f32[1024]{0:T(1024)} %param.18) | copy-start | bytes 12292
  125.6 36.5 %reduce-scatter.5.cloned.1.call-start = ((), (), s32[]{:S(2)}) async-start(), calls=%async_computation.6 | async-start | bytes 1572864 | tf_op jit(solution)/shard_map/reduce_scatter | solution.py:98
  145.6 3.0 copy-start.16
  148.6 25.2 %copy-start.7 = (bf16[1024,512]{1,0:T(8,128)(2,1)S(1)}, bf16[1024,512]{1,0:T(8,128)(2,1)}, u32[]{:S(2)}) copy-start(bf16[1024,512]{1,0:T(8,128)(2,1)} %param.15) | copy-start | bytes 3145732
  152.3 21.5 %all-gather.6.cloned.1.call-start = ((), (), s32[]{:S(2)}) async-start(), calls=%async_computation.7 | async-start | bytes 1572864 | tf_op jit(solution)/shard_map/all_gather | solution.py:106
  162.1 36.3 %all-reduce.35.cloned.1.call-start = ((), (), s32[]{:S(2)}) async-start(), calls=%async_computation.8 | async-start | bytes 2097152 | tf_op jit(solution)/shard_map/psum | solution.py:91
  175.9 24.0 %copy-start.13 = (bf16[1024,512]{1,0:T(8,128)(2,1)S(1)}, bf16[1024,512]{1,0:T(8,128)(2,1)}, u32[]{:S(2)}) copy-start(bf16[1024,512]{1,0:T(8,128)(2,1)} %param.19) | copy-start | bytes 3145732
  177.7 38.6 %reduce-scatter.7.cloned.1.call-start = ((), (), s32[]{:S(2)}) async-start(), calls=%async_computation.9 | async-start | bytes 1572864 | tf_op jit(solution)/shard_map/reduce_scatter | solution.py:98
  206.5 21.4 %all-gather.8.cloned.1.call-start = ((), (), s32[]{:S(2)}) async-start(), calls=%async_computation.10 | async-start | bytes 1572864 | tf_op jit(solution)/shard_map/all_gather | solution.py:106
  216.3 36.3 %all-reduce.37.cloned.1.call-start = ((), (), s32[]{:S(2)}) async-start(), calls=%async_computation.11 | async-start | bytes 2097152 | tf_op jit(solution)/shard_map/psum | solution.py:91
  230.1 24.0 %copy-start.14 = (bf16[1024,512]{1,0:T(8,128)(2,1)S(1)}, bf16[1024,512]{1,0:T(8,128)(2,1)}, u32[]{:S(2)}) copy-start(bf16[1024,512]{1,0:T(8,128)(2,1)} %param.19) | copy-start | bytes 3145732
  231.8 38.7 %reduce-scatter.9.cloned.1.call-start = ((), (), s32[]{:S(2)}) async-start(), calls=%async_computation.12 | async-start | bytes 1572864 | tf_op jit(solution)/shard_map/reduce_scatter | solution.py:98
  257.1 25.2 %copy-start.8 = (bf16[1024,512]{1,0:T(8,128)(2,1)S(1)}, bf16[1024,512]{1,0:T(8,128)(2,1)}, u32[]{:S(2)}) copy-start(bf16[1024,512]{1,0:T(8,128)(2,1)} %param.15) | copy-start | bytes 3145732
  260.8 21.5 %all-gather.10.cloned.1.call-start = ((), (), s32[]{:S(2)}) async-start(), calls=%async_computation.13 | async-start | bytes 1572864 | tf_op jit(solution)/shard_map/all_gather | solution.py:106
  270.5 36.0 %all-reduce.39.cloned.1.call-start = ((), (), s32[]{:S(2)}) async-start(), calls=%async_computation.14 | async-start | bytes 2097152 | tf_op jit(solution)/shard_map/psum | solution.py:91
  285.7 22.3 %copy-start.15 = (bf16[1024,512]{1,0:T(8,128)(2,1)S(1)}, bf16[1024,512]{1,0:T(8,128)(2,1)}, u32[]{:S(2)}) copy-start(bf16[1024,512]{1,0:T(8,128)(2,1)} %param.19) | copy-start | bytes 3145732
  285.8 38.6 %reduce-scatter.11.cloned.1.call-start = ((), (), s32[]{:S(2)}) async-start(), calls=%async_computation.15 | async-start | bytes 1572864 | tf_op jit(solution)/shard_map/reduce_scatter | solution.py:98
  311.0 3.7 %copy-start.2 = (bf16[512,512]{1,0:T(8,128)(2,1)S(1)}, bf16[512,512]{1,0:T(8,128)(2,1)}, u32[]{:S(2)}) copy-start(bf16[512,512]{1,0:T(8,128)(2,1)} %reduce-scatter.5.cloned.1.call-done) | copy-start | bytes 1572868
  314.7 3.2 copy-start.3
  324.4 2.2 copy-start.1
Sparse Core Ops, SparseCore 0:
  125.7 18.4 all-reduce.32
  152.5 9.5 reduce-scatter.4
  163.6 10.1 all-gather.5
  177.8 20.5 all-reduce.34
  206.6 9.5 reduce-scatter.6
  217.6 10.1 all-gather.7
  232.0 20.5 all-reduce.36
  260.9 9.5 reduce-scatter.8
  272.1 10.1 all-gather.9
  285.9 20.5 all-reduce.38
  314.8 9.5 reduce-scatter.10
where the time goes:
time: 340 us; the launch traced here: 339 us
  waiting for transfers between devices  149 us (44%)
  blocking collectives  78.5 us (23%)
  matrix products  41.5 us (12%)
  local copies, waits for them, and re-layouts  31.1 us (9%)
  other arithmetic  24 us (7%)
  between operations  14.1 us (4%)
    psum x4, waiting for transfers between devices, per_device(): lax.psum(jnp.dot(current.astype(jnp.bfloat16), readout_w, preferred_eleme...  80.3 us
    all_gather x2, blocking collectives, carried_in(): pieces = jax.tree.map(lambda part: lax.all_gather(part, axis), value)  63 us
    all_gather x3, waiting for transfers between devices, per_device(): full_guess = lax.all_gather(guessed, 'mp', axis=1, tiled=True)  35 us
    reduce_scatter x4, waiting for transfers between devices, per_device(): lax.psum_scatter(jnp.dot(hidden, w_out, preferred_element_type=jnp.float3...  33.6 us
    all_to_all x1, blocking collectives, per_device(): lax.all_to_all(shortened(corrected.reshape(batch, 1, steps, width_part)),...  15.5 us
    dot_general x4, matrix products, per_device(): jnp.dot(hidden, w_out, preferred_element_type=jnp.float32)  14.6 us
    pad x24, local copies, waits for them, and re-layouts, per_device(): lax.associative_scan(combine, (gates, driven), axis=1)  12.2 us
    dot_general x4, matrix products, hidden_units(): jnp.dot(normed, w_hidden, preferred_element_type=jnp.float32)  11.8 us
  transfers between devices with their start and end apart: 11, of which 11 were waited for; matrix products, arithmetic and copies ran while one was open for 2% of the time, Pallas kernels for 0%

commit v1 on v0

--- a/solution.py
+++ b/solution.py
@@ -88,11 +88,14 @@
     action_rows = actions.reshape(rows, horizon)
     outputs = []
     for step in range(horizon):
-        features = lax.psum(
-            jnp.dot(
-                current.astype(jnp.bfloat16), readout_w, preferred_element_type=jnp.float32
-            ).astype(jnp.bfloat16),
-            "mp",
+        features = jnp.sum(
+            lax.all_gather(
+                jnp.dot(
+                    current.astype(jnp.bfloat16), readout_w, preferred_element_type=jnp.float32
+                ).astype(jnp.bfloat16),
+                "mp",
+            ),
+            axis=0,
         ).astype(jnp.float32)
         hidden = hidden_units(features, norm_gain, w_hidden, action_embed, action_rows[:, step])
         guessed = lax.psum_scatter(

time: 340 us -> 306 us (0.900)
  waiting for transfers between devices: 149 us -> 113 us
  other arithmetic: 24 us -> 27.9 us
    psum x4 -> x0, waiting for transfers between devices: 80.3 us -> none  [per_device(): lax.psum(jnp.dot(current.astype(jnp.bfloat16), readout_w, preferred_eleme...]
    all_gather x0 -> x4, waiting for transfers between devices: none -> 44.7 us  [per_device(): lax.all_gather(jnp.dot(current.astype(jnp.bfloat16), readout_w, preferred...]
    reduce_sum x0 -> x4, other arithmetic: none -> 8.81 us  [per_device(): jnp.sum(lax.all_gather(jnp.dot(current.astype(jnp.bfloat16), readout_w, p...]
    reduce_sum x4, other arithmetic: 6.01 us -> 1.12 us  [hidden_units(): mean_sq = jnp.mean(features * features, axis=-1, keepdims=True)]
where the time goes in v1:
time: 306 us; the launch traced here: 305 us
  waiting for transfers between devices  113 us (37%)
  blocking collectives  78.5 us (26%)
  matrix products  39 us (13%)
  local copies, waits for them, and re-layouts  31.1 us (10%)
  other arithmetic  27.9 us (9%)
  between operations  14.1 us (5%)
    all_gather x2, blocking collectives, carried_in(): pieces = jax.tree.map(lambda part: lax.all_gather(part, axis), value)  63 us
    all_gather x4, waiting for transfers between devices, per_device(): lax.all_gather(jnp.dot(current.astype(jnp.bfloat16), readout_w, preferred...  44.7 us
    all_gather x3, waiting for transfers between devices, per_device(): full_guess = lax.all_gather(guessed, 'mp', axis=1, tiled=True)  35 us
    reduce_scatter x4, waiting for transfers between devices, per_device(): lax.psum_scatter(jnp.dot(hidden, w_out, preferred_element_type=jnp.float3...  33.5 us
    all_to_all x1, blocking collectives, per_device(): lax.all_to_all(shortened(corrected.reshape(batch, 1, steps, width_part)),...  15.5 us
    dot_general x4, matrix products, per_device(): jnp.dot(hidden, w_out, preferred_element_type=jnp.float32)  14.6 us
    pad x24, local copies, waits for them, and re-layouts, per_device(): lax.associative_scan(combine, (gates, driven), axis=1)  12.2 us
    dot_general x4, matrix products, hidden_units(): jnp.dot(normed, w_hidden, preferred_element_type=jnp.float32)  9.39 us
  transfers between devices with their start and end apart: 11, of which 11 were waited for; matrix products, arithmetic and copies ran while one was open for 2% of the time, Pallas kernels for 0%

profile of v1, /device:TPU:0, one launch (start us, length us, event | category | flops | bytes accessed | tf_op | source)
XLA Modules:
  0.0 304.9 jit_solution(11662835133420371287)
XLA Ops:
  6.5 0.8 subtract_convert_fusion
  7.3 0.8 subtract_sqrt_fusion
  8.8 1.5 slice.219
  10.3 2.2 convolution_multiply_fusion.3
  12.6 1.5 slice.268
  14.1 1.5 slice.222
  15.6 1.4 slice.221
  17.0 1.4 multiply_add_fusion
  19.3 0.8 slice.225
  22.9 0.5 copy-done.9
  24.1 0.9 add.272
  25.0 0.9 add.264
  25.9 1.2 fusion.36
  27.4 0.7 copy-done.6
  28.1 0.9 pad_maximum_fusion.1
  29.0 2.0 pad.98
  31.0 4.3 %pad.99 = f32[4,128,512]{2,1,0:T(8,128)} pad(f32[4,64,512]{2,1,0:T(8,128)} %add.264, f32[]{:T(128)} %constant.56.clone.1), padding=0_0_0x1_0_1x0_0_0 | pad | bytes 1572868 | tf_op jit(solution)/shard_map/pad | solution.py:70
  35.3 0.9 slice_add_fusion
  36.2 32.4 %all-gather.1 = f32[32,1,512]{2,1,0:T(1,128)S(1)} all-gather(f32[4,1,512]{2,1,0:T(1,128)S(1)} %slice_add_fusion), channel_id=3, replica_groups=mesh['rep'=2,'tm'=8,'mp'=2] {'tm'}, dimensions={0}, use_global_device_ids=true | all-gather | bytes 73728 | tf_op jit(solution)/shard_map/all_gather | solution.py:9
  68.7 4.3 %pad.113 = f32[4,128,512]{2,1,0:T(8,128)} pad(f32[4,64,512]{2,1,0:T(8,128)} %add.272, f32[]{:T(128)} %constant.56.clone.1), padding=0_0_0x1_0_1x0_0_0 | pad | bytes 1572868 | tf_op jit(solution)/shard_map/pad | solution.py:70
  73.0 0.9 slice_add_fusion.1
  73.8 30.7 %all-gather = f32[32,1,512]{2,1,0:T(1,128)S(1)} all-gather(f32[4,1,512]{2,1,0:T(1,128)S(1)} %slice_add_fusion.1), channel_id=2, replica_groups=mesh['rep'=2,'tm'=8,'mp'=2] {'tm'}, dimensions={0}, use_global_device_ids=true | all-gather | bytes 73728 | tf_op jit(solution)/shard_map/all_gather | solution.py:9
  104.7 0.3 while.14
  105.0 2.0 fusion.35
  107.0 0.4 copy.27
  107.5 15.5 %all_to_all.4 = bf16[4,1,128,512]{3,0,1,2:T(4,128)(2,1)S(1)} all-to-all(bf16[4,1,128,512]{3,0,1,2:T(4,128)(2,1)S(1)} %copy.27), channel_id=1, replica_groups=mesh['rep'=2,'tm'=8,'mp'=2] {'tm'}, dimensions={2} | all-to-all | bytes 1048576 | tf_op jit(solution)/shard_map/all_to_all | solution.py:78
  123.1 0.8 copy-done.10
  123.8 1.7 convolution_convert_fusion.7
  125.7 9.5 %all-gather.20.cloned.1.call-done = bf16[1024,1024]{1,0:T(8,128)(2,1)} async-done(((bf16[512,1024]{1,0:T(8,128)(2,1)}), bf16[1024,1024]{1,0:T(8,128)(2,1)}) %all-gather.20.cloned.1.call-update) | async-done | bytes 2097168 | tf_op jit(solution)/shard_map/all_gather | solution.py:92
  135.3 2.2 reduce_sum.84
  137.5 0.3 fusion.1
  137.8 1.7 fusion.23
  139.6 3.7 %convolution_convert_fusion.6 = bf16[512,1024]{1,0:T(8,128)(2,1)} fusion(bf16[512,1024]{1,0:T(8,128)(2,1)} %param.21, f32[512,512]{1,0:T(8,128)} %fusion.23, bf16[18,512]{1,0:T(8,128)(2,1)S(1)} %copy-done.14, s32[512]{0:T(512)S(1)} %bitcast.99), kind=kOutput, calls=%fused_computation.30 | convolution fusion | flops 548414464 | bytes 3166208 | tf_op jit(solution)/shard_map/dot_general | solution.py:102
  143.3 9.7 %reduce-scatter.5.cloned.1.call-done = bf16[512,512]{1,0:T(8,128)(2,1)} async-done(((bf16[512,1024]{1,0:T(8,128)(2,1)}), bf16[512,512]{1,0:T(8,128)(2,1)}) %reduce-scatter.5.cloned.1.call-update) | async-done | bytes 524304 | tf_op jit(solution)/shard_map/reduce_scatter | solution.py:101
  153.1 11.7 %all-gather.14.cloned.1.call-done = bf16[512,1024]{1,0:T(8,128)(2,1)} async-done(((bf16[512,512]{1,0:T(8,128)(2,1)}), bf16[512,1024]{1,0:T(8,128)(2,1)}) %all-gather.14.cloned.1.call-update) | async-done | bytes 1048592 | tf_op jit(solution)/shard_map/all_gather | solution.py:109
  164.8 2.1 fusion.15
  166.8 1.7 convolution_convert_fusion.5
  168.8 11.7 %all-gather.22.cloned.1.call-done = bf16[1024,1024]{1,0:T(8,128)(2,1)} async-done(((bf16[512,1024]{1,0:T(8,128)(2,1)}), bf16[1024,1024]{1,0:T(8,128)(2,1)}) %all-gather.22.cloned.1.call-update) | async-done | bytes 2097168 | tf_op jit(solution)/shard_map/all_gather | solution.py:92
  180.5 2.2 reduce_sum.86
  182.9 3.0 fusion.21
  185.9 3.6 %convolution_convert_fusion.4 = bf16[512,1024]{1,0:T(8,128)(2,1)} fusion(bf16[512,1024]{1,0:T(8,128)(2,1)} %param.21, f32[512,512]{1,0:T(8,128)} %fusion.21, bf16[18,512]{1,0:T(8,128)(2,1)S(1)} %copy-done.14, s32[512]{0:T(512)S(1)} %bitcast.98), kind=kOutput, calls=%fused_computation.28 | convolution fusion | flops 548414464 | bytes 3166208 | tf_op jit(solution)/shard_map/dot_general | solution.py:102
  189.5 9.7 %reduce-scatter.7.cloned.1.call-done = bf16[512,512]{1,0:T(8,128)(2,1)} async-done(((bf16[512,1024]{1,0:T(8,128)(2,1)}), bf16[512,512]{1,0:T(8,128)(2,1)}) %reduce-scatter.7.cloned.1.call-update) | async-done | bytes 524304 | tf_op jit(solution)/shard_map/reduce_scatter | solution.py:101
  199.2 11.6 %all-gather.16.cloned.1.call-done = bf16[512,1024]{1,0:T(8,128)(2,1)} async-done(((bf16[512,512]{1,0:T(8,128)(2,1)}), bf16[512,1024]{1,0:T(8,128)(2,1)}) %all-gather.16.cloned.1.call-update) | async-done | bytes 1048592 | tf_op jit(solution)/shard_map/all_gather | solution.py:109
  210.8 2.2 fusion.14
  213.1 1.7 convolution_convert_fusion.3
  214.8 11.9 %all-gather.24.cloned.1.call-done = bf16[1024,1024]{1,0:T(8,128)(2,1)} async-done(((bf16[512,1024]{1,0:T(8,128)(2,1)}), bf16[1024,1024]{1,0:T(8,128)(2,1)}) %all-gather.24.cloned.1.call-update) | async-done | bytes 2097168 | tf_op jit(solution)/shard_map/all_gather | solution.py:92
  226.7 2.2 reduce_sum.88
  228.8 0.3 fusion.7
  229.1 3.0 fusion.19
  232.1 3.7 %convolution_convert_fusion.2 = bf16[512,1024]{1,0:T(8,128)(2,1)} fusion(bf16[512,1024]{1,0:T(8,128)(2,1)} %param.21, f32[512,512]{1,0:T(8,128)} %fusion.19, bf16[18,512]{1,0:T(8,128)(2,1)S(1)} %copy-done.14, s32[512]{0:T(512)S(1)} %bitcast.97), kind=kOutput, calls=%fused_computation.26 | convolution fusion | flops 548414464 | bytes 3166208 | tf_op jit(solution)/shard_map/dot_general | solution.py:102
  235.8 9.7 %reduce-scatter.9.cloned.1.call-done = bf16[512,512]{1,0:T(8,128)(2,1)} async-done(((bf16[512,1024]{1,0:T(8,128)(2,1)}), bf16[512,512]{1,0:T(8,128)(2,1)}) %reduce-scatter.9.cloned.1.call-update) | async-done | bytes 524304 | tf_op jit(solution)/shard_map/reduce_scatter | solution.py:101
  245.6 11.7 %all-gather.18.cloned.1.call-done = bf16[512,1024]{1,0:T(8,128)(2,1)} async-done(((bf16[512,512]{1,0:T(8,128)(2,1)}), bf16[512,1024]{1,0:T(8,128)(2,1)}) %all-gather.18.cloned.1.call-update) | async-done | bytes 1048592 | tf_op jit(solution)/shard_map/all_gather | solution.py:109
  257.3 3.5 %convolution_convert_fusion.1 = bf16[512,1024]{1,0:T(8,128)(2,1)} fusion(bf16[512,1024]{1,0:T(8,128)(2,1)S(1)} %copy-done, bf16[512,1024]{1,0:T(8,128)(2,1)} %all-gather.18.cloned.1.call-done, bf16[1024,512]{1,0:T(8,128)(2,1)S(1)} %copy-done.8, f32[512,512]{1,0:T(8,128)S(1)} %fusion.14, f32[512]{0:T(512)S(1)} %get-tuple-element.128, ...), kind=kOutput, calls=%fused_computation.25 | convolution fusion | flops 1075314688 | bytes 5246976 | tf_op jit(solution)/shard_map/dot_general | solution.py:93
  261.0 11.6 %all-gather.26.cloned.1.call-done = bf16[1024,1024]{1,0:T(8,128)(2,1)} async-done(((bf16[512,1024]{1,0:T(8,128)(2,1)}), bf16[1024,1024]{1,0:T(8,128)(2,1)}) %all-gather.26.cloned.1.call-update) | async-done | bytes 2097168 | tf_op jit(solution)/shard_map/all_gather | solution.py:92
  272.7 2.2 reduce_sum.90
  274.9 0.3 fusion.10
  275.2 1.7 fusion.17
  277.0 3.6 %convolution_convert_fusion = bf16[512,1024]{1,0:T(8,128)(2,1)} fusion(bf16[512,1024]{1,0:T(8,128)(2,1)} %param.21, f32[512,512]{1,0:T(8,128)} %fusion.17, bf16[18,512]{1,0:T(8,128)(2,1)S(1)} %copy-done.14, s32[512]{0:T(512)S(1)} %bitcast.96), kind=kOutput, calls=%fused_computation.24 | convolution fusion | flops 548414464 | bytes 3166208 | tf_op jit(solution)/shard_map/dot_general | solution.py:102
  280.7 1.0 copy.30
  281.7 2.1 copy.31
  283.8 2.0 copy.32
  285.8 4.5 %reduce-scatter.11.cloned.1.call-done = bf16[512,512]{1,0:T(8,128)(2,1)} async-done(((bf16[512,1024]{1,0:T(8,128)(2,1)}), bf16[512,512]{1,0:T(8,128)(2,1)}) %reduce-scatter.11.cloned.1.call-update) | async-done | bytes 524304 | tf_op jit(solution)/shard_map/reduce_scatter | solution.py:101
  290.3 2.2 copy.33
  292.5 5.9 %pad_maximum_fusion = bf16[4,8,16,4,512]{4,3,2,1,0:T(4,128)(2,1)} fusion(bf16[4,8,16,1,512]{4,3,2,1,0:T(2,128)(2,1)S(1)} %copy.33, bf16[4,8,16,1,512]{4,3,2,1,0:T(2,128)(2,1)S(1)} %copy-done.1, bf16[4,8,16,1,512]{4,3,2,1,0:T(2,128)(2,1)S(1)} %copy.31, bf16[4,8,16,1,512]{4,3,2,1,0:T(2,128)(2,1)S(1)} %copy.30), kind=kLoop, calls=%fused_computation.23 | loop fusion | flops 8388608 | bytes 4194304 | tf_op jit(solution)/shard_map/stack | solution.py:113
  (163 shorter events, 6.9 us)
Async XLA Ops:
  6.5 117.3 %copy-start = (bf16[512,1024]{1,0:T(8,128)(2,1)S(1)}, bf16[512,1024]{1,0:T(8,128)(2,1)}, u32[]{:S(2)}) copy-start(bf16[512,1024]{1,0:T(8,128)(2,1)} %param.17) | copy-start | bytes 3145732
  6.5 128.7 %all-gather.20.cloned.1.call-start = ((), (), s32[]{:S(2)}) async-start(), calls=%async_computation.12 | async-start | bytes 3145728 | tf_op jit(solution)/shard_map/all_gather | solution.py:92
  22.4 1.0 copy-start.9
  24.1 1.8 copy-start.4
  24.1 1.8 copy-start.5
  27.0 1.0 copy-start.6
  123.0 0.8 copy-start.10
  123.0 2.5 copy-start.11
  125.5 27.4 %reduce-scatter.5.cloned.1.call-start = ((), (), s32[]{:S(2)}) async-start(), calls=%async_computation.5 | async-start | bytes 1572864 | tf_op jit(solution)/shard_map/reduce_scatter | solution.py:101
  135.3 2.6 copy-start.12
  135.3 2.6 copy-start.15
  137.8 1.8 copy-start.14
  139.6 25.2 %copy-start.7 = (bf16[1024,512]{1,0:T(8,128)(2,1)S(1)}, bf16[1024,512]{1,0:T(8,128)(2,1)}, u32[]{:S(2)}) copy-start(bf16[1024,512]{1,0:T(8,128)(2,1)} %param.15) | copy-start | bytes 3145732
  143.3 21.5 %all-gather.14.cloned.1.call-start = ((), (), s32[]{:S(2)}) async-start(), calls=%async_computation.6 | async-start | bytes 1572864 | tf_op jit(solution)/shard_map/all_gather | solution.py:109
  153.0 27.5 %all-gather.22.cloned.1.call-start = ((), (), s32[]{:S(2)}) async-start(), calls=%async_computation.13 | async-start | bytes 3145728 | tf_op jit(solution)/shard_map/all_gather | solution.py:92
  168.6 30.6 %reduce-scatter.7.cloned.1.call-start = ((), (), s32[]{:S(2)}) async-start(), calls=%async_computation.7 | async-start | bytes 1572864 | tf_op jit(solution)/shard_map/reduce_scatter | solution.py:101
  189.5 21.3 %all-gather.16.cloned.1.call-start = ((), (), s32[]{:S(2)}) async-start(), calls=%async_computation.8 | async-start | bytes 1572864 | tf_op jit(solution)/shard_map/all_gather | solution.py:109
  199.2 27.5 %all-gather.24.cloned.1.call-start = ((), (), s32[]{:S(2)}) async-start(), calls=%async_computation.14 | async-start | bytes 3145728 | tf_op jit(solution)/shard_map/all_gather | solution.py:92
  214.8 30.7 %reduce-scatter.9.cloned.1.call-start = ((), (), s32[]{:S(2)}) async-start(), calls=%async_computation.9 | async-start | bytes 1572864 | tf_op jit(solution)/shard_map/reduce_scatter | solution.py:101
  232.1 25.2 %copy-start.8 = (bf16[1024,512]{1,0:T(8,128)(2,1)S(1)}, bf16[1024,512]{1,0:T(8,128)(2,1)}, u32[]{:S(2)}) copy-start(bf16[1024,512]{1,0:T(8,128)(2,1)} %param.15) | copy-start | bytes 3145732
  235.8 21.5 %all-gather.18.cloned.1.call-start = ((), (), s32[]{:S(2)}) async-start(), calls=%async_computation.10 | async-start | bytes 1572864 | tf_op jit(solution)/shard_map/all_gather | solution.py:109
  245.5 27.2 %all-gather.26.cloned.1.call-start = ((), (), s32[]{:S(2)}) async-start(), calls=%async_computation.15 | async-start | bytes 3145728 | tf_op jit(solution)/shard_map/all_gather | solution.py:92
  260.8 29.6 %reduce-scatter.11.cloned.1.call-start = ((), (), s32[]{:S(2)}) async-start(), calls=%async_computation.11 | async-start | bytes 1572864 | tf_op jit(solution)/shard_map/reduce_scatter | solution.py:101
  272.7 2.5 copy-start.13
  277.0 3.7 %copy-start.2 = (bf16[512,512]{1,0:T(8,128)(2,1)S(1)}, bf16[512,512]{1,0:T(8,128)(2,1)}, u32[]{:S(2)}) copy-start(bf16[512,512]{1,0:T(8,128)(2,1)} %reduce-scatter.5.cloned.1.call-done) | copy-start | bytes 1572868
  280.6 3.2 %copy-start.3 = (bf16[512,512]{1,0:T(8,128)(2,1)S(1)}, bf16[512,512]{1,0:T(8,128)(2,1)}, u32[]{:S(2)}) copy-start(bf16[512,512]{1,0:T(8,128)(2,1)} %reduce-scatter.9.cloned.1.call-done) | copy-start | bytes 1572868
  290.3 2.2 copy-start.1
Sparse Core Ops, SparseCore 0:
  125.7 9.5 all-gather.19
  143.4 9.5 reduce-scatter.4
  154.5 10.1 all-gather.13
  168.7 11.7 all-gather.21
  189.6 9.5 reduce-scatter.6
  200.6 10.1 all-gather.15
  214.9 11.7 all-gather.23
  235.9 9.5 reduce-scatter.8
  247.0 10.1 all-gather.17
  260.9 11.7 all-gather.25
  280.8 9.5 reduce-scatter.10
